TPU v7x, 32 devices: a whole 2x2x4 slice. The times are simulated.
32 devices in a mesh: dp: 4 (over y, x), expert: 8 (over z, core).
Axes of the slice: x: 2, y: 2, z: 4, core: 2. Of those that a mesh axis runs over, the one named last changes fastest.
Arguments:
- tokens: bfloat16 [4096, 7168], P(('dp', 'expert')), may hold values from -6 to 6
- steering: float32 [7168], replicated, may hold values from -6 to 6
- norm_gain: float32 [7168], replicated, may hold values from 0.1 to 1.9
- route_ids: int32 [4096, 8], P(('dp', 'expert')), may hold values from 0 to 255, as said below
- route_gates: int32 [4096, 8], P(('dp', 'expert')), may hold values from 1 to 65535
- gate_weight: bfloat16 [7168, 8192], P(None, 'expert'), may hold values from -0.0625 to 0.0625
- up_weight: bfloat16 [7168, 8192], P(None, 'expert'), may hold values from -0.0625 to 0.0625
- down_weight: bfloat16 [8192, 7168], P('expert'), may hold values from -0.125 to 0.125
- out_grad: bfloat16 [4096, 7168], P(('dp', 'expert')), may hold values from -6 to 6
Outputs:
- layer_out: bfloat16 [4096, 7168], P(('dp', 'expert'))
- in_grad: bfloat16 [4096, 7168], P(('dp', 'expert'))
- steer_grad: float32 [7168], replicated
Inputs may be any that keep to these rules, and one draw needn't show every extreme that they name: `route_ids`: each row names 8 different experts. Among the 128 rows of one device no expert below 4 is named more than 8 times. One expert below 4, the same for every device, is named exactly 8 times by every device's rows, and on some devices every expert below 4 is named exactly 8 times.
All inputs are finite; a program needn't handle non-finite values.
Results may differ from a plain program's by a relative error of at most 0.0021.
Values may be sent and summed in bfloat16 or wider, within the bound.
No kernel may reach another device: no remote copies, remote signals or barrier semaphores. Data moves between devices by JAX's collectives and lax.ppermute only.
A program may use at most 128 MiB of HBM per device.

v0:
```python
import jax
import jax.numpy as jnp
from jax import lax
from jax.sharding import PartitionSpec as P

EXP_FLIGHT = 4
CAP = 8
EPSILON = 1e-06
GATE_UNIT = 1.0 / 65536.0


def slot_tables(route_ids, route_gates, flight, capacity):
    count_rows = route_ids.shape[0]
    expert_range = jnp.arange(flight, dtype=jnp.int32)
    hit_mask = route_ids[:, :, None] == expert_range[None, None, :]
    member = jnp.any(hit_mask, axis=1)
    scaled = route_gates.astype(jnp.float32) * GATE_UNIT
    weights = jnp.sum(jnp.where(hit_mask, scaled[:, :, None], 0.0), axis=1)
    position = jnp.cumsum(member.astype(jnp.int32), axis=0) - 1
    slot_of = jnp.where(member, position, capacity)
    slot_range = jnp.arange(capacity, dtype=jnp.int32)
    matches = slot_of[:, :, None] == slot_range[None, None, :]
    row_range = jnp.arange(count_rows, dtype=jnp.int32)
    slot_table = jnp.sum(jnp.where(matches, row_range[:, None, None], 0), axis=0)
    filled = jnp.any(matches, axis=0)
    combine = jnp.where(matches, weights[:, :, None], 0.0).reshape(count_rows, flight * capacity)
    return (slot_table, filled, combine)


def dispatch_rows(values, slot_table, filled):
    picked = values[slot_table]
    return jnp.where(filled[:, :, None], picked, jnp.zeros((), values.dtype))


def normalize(tokens, steering, norm_gain):
    residual = tokens.astype(jnp.float32) + steering
    inverse = lax.rsqrt(jnp.mean(residual * residual, axis=-1, keepdims=True) + EPSILON)
    normed = (residual * inverse * norm_gain).astype(jnp.bfloat16)
    return (residual, inverse, normed)


def norm_backward(residual, inverse, norm_gain, back_normed, out_grad):
    scaled = back_normed * norm_gain
    inner_mean = jnp.mean(scaled * residual, axis=-1, keepdims=True)
    cubed = inverse * inverse * inverse
    return out_grad.astype(jnp.float32) + inverse * scaled - residual * cubed * inner_mean


def share_forward(token_rows, gate_cols, up_cols, down_rows):
    gate_pre = jnp.dot(token_rows, gate_cols, preferred_element_type=jnp.float32)
    up_pre = jnp.dot(token_rows, up_cols, preferred_element_type=jnp.float32)
    hidden = (jax.nn.silu(gate_pre) * up_pre).astype(jnp.bfloat16)
    forward = jnp.dot(hidden, down_rows, preferred_element_type=jnp.float32).astype(jnp.bfloat16)
    return (forward, gate_pre, up_pre)


def share_backward(grad_rows, gate_pre, up_pre, gate_cols, up_cols, down_rows):
    contract = (((1,), (1,)), ((), ()))
    back_hidden = lax.dot_general(
        grad_rows, down_rows, contract, preferred_element_type=jnp.float32
    )
    sigmoid = jax.nn.sigmoid(gate_pre)
    back_up = (back_hidden * gate_pre * sigmoid).astype(jnp.bfloat16)
    back_gate = (back_hidden * up_pre * sigmoid * (1.0 + gate_pre * (1.0 - sigmoid))).astype(
        jnp.bfloat16
    )
    backward = lax.dot_general(back_gate, gate_cols, contract, preferred_element_type=jnp.float32)
    backward = backward + lax.dot_general(
        back_up, up_cols, contract, preferred_element_type=jnp.float32
    )
    return backward.astype(jnp.bfloat16)


def apply_combine(combine, partial_sums):
    return jnp.dot(combine, partial_sums, precision=lax.Precision.HIGHEST)


def shards(
    tokens,
    steering,
    norm_gain,
    route_ids,
    route_gates,
    gate_weight,
    up_weight,
    down_weight,
    out_grad,
):
    expert_count = lax.axis_size("expert")
    flight = EXP_FLIGHT
    group_size = expert_count // flight
    capacity = CAP
    feature_count = tokens.shape[1]
    residual, inverse, normed = normalize(tokens, steering, norm_gain)
    slot_table, filled, combine = slot_tables(route_ids, route_gates, flight, capacity)
    packed = jnp.stack(
        [dispatch_rows(normed, slot_table, filled), dispatch_rows(out_grad, slot_table, filled)],
        axis=1,
    )
    sending = jnp.repeat(packed, group_size, axis=0)
    arrived = lax.all_to_all(sending, "expert", split_axis=0, concat_axis=0, tiled=True)
    local_rows = arrived[:, 0].reshape(expert_count * capacity, feature_count)
    local_grads = arrived[:, 1].reshape(expert_count * capacity, feature_count)
    forward, gate_pre, up_pre = share_forward(local_rows, gate_weight, up_weight, down_weight)
    came_out = lax.all_to_all(
        forward.reshape(expert_count, capacity, feature_count),
        "expert",
        split_axis=0,
        concat_axis=0,
        tiled=True,
    )
    backward = share_backward(local_grads, gate_pre, up_pre, gate_weight, up_weight, down_weight)
    came_grad = lax.all_to_all(
        backward.reshape(expert_count, capacity, feature_count),
        "expert",
        split_axis=0,
        concat_axis=0,
        tiled=True,
    )
    out_sums = (
        came_out.reshape(flight, group_size, capacity, feature_count)
        .astype(jnp.float32)
        .sum(axis=1)
    )
    grad_sums = (
        came_grad.reshape(flight, group_size, capacity, feature_count)
        .astype(jnp.float32)
        .sum(axis=1)
    )
    mixture = apply_combine(combine, out_sums.reshape(flight * capacity, feature_count))
    back_normed = apply_combine(combine, grad_sums.reshape(flight * capacity, feature_count))
    layer_out = (residual + mixture).astype(jnp.bfloat16)
    total_grad = norm_backward(residual, inverse, norm_gain, back_normed, out_grad)
    steer_grad = lax.psum(jnp.sum(total_grad, axis=0), ("dp", "expert"))
    return (layer_out, total_grad.astype(jnp.bfloat16), steer_grad)


def solution(mesh):
    in_specs = (
        P(("dp", "expert"), None),
        P(),
        P(),
        P(("dp", "expert"), None),
        P(("dp", "expert"), None),
        P(None, "expert"),
        P(None, "expert"),
        P("expert", None),
        P(("dp", "expert"), None),
    )
    out_specs = (P(("dp", "expert"), None), P(("dp", "expert"), None), P())
    return jax.shard_map(shards, mesh=mesh, in_specs=in_specs, out_specs=out_specs, check_vma=False)
```

profile of v0, /device:TPU:0, one launch (start us, length us, event | category | flops | bytes accessed | tf_op | source)
XLA Modules:
  0.0 191.6 jit_solution(9282980750656883561)
XLA Ops:
  0.6 0.7 fusion.16
  1.3 0.1 copy.20
  1.5 0.2 reduce_window_sum.11
  1.6 0.1 copy.21
  1.7 0.2 select_reduce_fusion
  1.9 0.2 fusion.15
  2.0 0.1 reshape.94
  2.1 2.1 %multiply_reduce_fusion.1 = f32[128]{0:T(128)S(1)} fusion(bf16[128,7168]{1,0:T(8,128)(2,1)} %param.9, f32[7168]{0:T(1024)} %param.10), kind=kLoop, calls=%fused_computation.15 | loop fusion | flops 3669888 | bytes 1864192 | tf_op jit(solution)/shard_map/reduce_sum | solution.py:37
  4.2 2.1 %multiply_convert_fusion = bf16[128,7168]{1,0:T(8,128)(2,1)S(1)} fusion(bf16[128,7168]{1,0:T(8,128)(2,1)} %param.9, f32[7168]{0:T(1024)} %param.11, f32[128]{0:T(128)S(1)} %get-tuple-element.6, f32[7168]{0:T(1024)} %param.10), kind=kLoop, calls=%fused_computation.14 | loop fusion | flops 4587520 | bytes 3727872 | tf_op jit(solution)/shard_map/convert_element_type | solution.py:38
  6.3 0.8 gather_fusion
  7.1 3.0 %gather_fusion.1 = bf16[32,7168]{1,0:T(8,128)(2,1)S(1)} fusion(bf16[128,7168]{1,0:T(8,128)(2,1)} %param.17, s32[1024]{0:T(1024)S(1)} %pad_clamp_fusion), kind=kCustom, calls=%fused_computation.1 | custom fusion | bytes 917632 | tf_op jit(solution)/shard_map/gather | solution.py:31
  10.1 0.1 bitcast_select_fusion.1
  10.3 0.1 pad_maximum_fusion
  10.4 0.1 copy.22
  10.4 0.2 broadcast_in_dim.84
  10.6 49.6 %all_to_all.15 = bf16[8,2,8,7168]{3,2,1,0:T(8,128)(2,1)S(1)} all-to-all(bf16[8,2,8,7168]{3,2,1,0:T(8,128)(2,1)S(1)} %bitcast.44), channel_id=1, replica_groups=mesh['dp'=4,'expert'=8] {'expert'}, dimensions={0} | all-to-all | bytes 3670016 | tf_op jit(solution)/shard_map/all_to_all | solution.py:101
  60.2 7.9 %fusion.8 = f32[64,1024]{1,0:T(8,128)S(1)} fusion(bf16[7168,1024]{1,0:T(8,128)(2,1)} %param.14, bf16[8,2,8,7168]{3,2,1,0:T(8,128)(2,1)S(1)} %all_to_all.15), kind=kOutput, calls=%fused_computation.24 | convolution fusion | flops 939524096 | bytes 15859712 | tf_op jit(solution)/shard_map/dot_general | solution.py:50
  68.0 9.7 %fusion.6 = f32[64,1024]{1,0:T(8,128)S(1)} fusion(bf16[1024,7168]{1,0:T(8,128)(2,1)} %param.16, bf16[8,2,8,7168]{3,2,1,0:T(8,128)(2,1)S(1)} %all_to_all.15), kind=kOutput, calls=%fused_computation.20 | convolution fusion | flops 939524096 | bytes 15859712 | tf_op jit(solution)/shard_map/dot_general | solution.py:59
  77.8 7.9 %fusion.7 = f32[64,1024]{1,0:T(8,128)S(1)} fusion(bf16[7168,1024]{1,0:T(8,128)(2,1)} %param.15, bf16[8,2,8,7168]{3,2,1,0:T(8,128)(2,1)S(1)} %all_to_all.15), kind=kOutput, calls=%fused_computation.23 | convolution fusion | flops 939524096 | bytes 15859712 | tf_op jit(solution)/shard_map/dot_general | solution.py:51
  85.6 9.7 %fusion.9 = f32[64,7168]{1,0:T(8,128)S(1)} fusion(bf16[7168,1024]{1,0:T(8,128)(2,1)} %param.14, f32[64,1024]{1,0:T(8,128)S(1)} %fusion.8, f32[64,1024]{1,0:T(8,128)S(1)} %fusion.6, f32[64,1024]{1,0:T(8,128)S(1)} %fusion.7), kind=kOutput, calls=%fused_computation.31 | convolution fusion | flops 940179456 | bytes 17301504 | tf_op jit(solution)/shard_map/dot_general | solution.py:67
  95.4 10.9 %fusion.5 = bf16[8,8,7168]{2,1,0:T(8,128)(2,1)} fusion(f32[64,7168]{1,0:T(8,128)S(1)} %fusion.9, bf16[7168,1024]{1,0:T(8,128)(2,1)} %param.15, f32[64,1024]{1,0:T(8,128)S(1)} %fusion.6, f32[64,1024]{1,0:T(8,128)S(1)} %fusion.8), kind=kOutput, calls=%fused_computation.11 | convolution fusion | flops 940834816 | bytes 17956864 | tf_op jit(solution)/shard_map/dot_general | solution.py:68
  106.3 3.6 %all-to-all-start.2 = ((bf16[8,8,7168]{2,1,0:T(8,128)(2,1)}), bf16[8,8,7168]{2,1,0:T(8,128)(2,1)S(1)}, u32[]{:S(2)}, u32[]{:S(2)}) async-start(bf16[8,8,7168]{2,1,0:T(8,128)(2,1)} %fusion.5), calls=%async_computation.2 | async-start | bytes 1835008 | tf_op jit(solution)/shard_map/all_to_all | solution.py:113
  109.8 0.0 copy-start.6
  109.8 0.0 copy-start.5
  109.9 8.8 %fusion.4 = bf16[8,8,7168]{2,1,0:T(8,128)(2,1)} fusion(bf16[1024,7168]{1,0:T(8,128)(2,1)} %param.16, f32[64,1024]{1,0:T(8,128)S(1)} %fusion.7, f32[64,1024]{1,0:T(8,128)S(1)} %fusion.8), kind=kOutput, calls=%fused_computation.10 | convolution fusion | flops 940376064 | bytes 16121856 | tf_op jit(solution)/shard_map/dot_general | solution.py:53
  118.6 0.0 copy-start
  118.6 0.0 copy-start.3
  118.6 0.0 copy-start.4
  118.6 14.9 %all-to-all-done.2 = bf16[8,8,7168]{2,1,0:T(8,128)(2,1)S(1)} async-done(((bf16[8,8,7168]{2,1,0:T(8,128)(2,1)}), bf16[8,8,7168]{2,1,0:T(8,128)(2,1)S(1)}, u32[]{:S(2)}, u32[]{:S(2)}) %all-to-all-start.2) | async-done | bytes 917536 | tf_op jit(solution)/shard_map/all_to_all | solution.py:113
  133.5 0.0 copy-start.2
  133.5 0.9 copy-done.2
  134.4 3.6 %all-to-all-start.1 = ((bf16[8,8,7168]{2,1,0:T(8,128)(2,1)}), bf16[8,8,7168]{2,1,0:T(8,128)(2,1)S(1)}, u32[]{:S(2)}, u32[]{:S(2)}) async-start(bf16[8,8,7168]{2,1,0:T(8,128)(2,1)} %fusion.4), calls=%async_computation.1 | async-start | bytes 1835008 | tf_op jit(solution)/shard_map/all_to_all | solution.py:105
  138.0 0.0 copy-done.6
  138.0 0.0 copy-done.5
  138.1 1.4 convert_reduce_fusion
  139.5 0.0 copy-done
  139.5 0.0 copy-done.3
  139.5 0.0 copy-done.4
  139.5 0.0 copy-start.1
  139.5 3.6 %multiply_reduce_fusion = (f32[128]{0:T(128)S(1)}, f32[128,7168]{1,0:T(8,128)S(1)}) fusion(bf16[128,7168]{1,0:T(8,128)(2,1)S(1)} %copy-done, f32[7168]{0:T(1024)S(1)} %copy-done.3, f32[7168]{0:T(1024)S(1)} %copy-done.4, f32[4,8,7168]{2,1,0:T(8,128)S(1)} %convert_reduce_fusion, f32[128,4]{0,1:T(4,128)S(1)} %select_reduce_fusion.1, ...), kind=kOutput, calls=%fused_computation.13 | convolution fusion | flops 356917120 | bytes 6484480 | tf_op jit(solution)/shard_map/dot_general | solution.py:75
  143.2 0.0 copy-done.1
  143.2 2.6 %fusion.28 = (f32[7168]{0:T(1024)S(1)}, bf16[128,7168]{1,0:T(8,128)(2,1)}) fusion(f32[128]{0:T(128)S(1)} %broadcast_multiply_fusion, f32[128]{0:T(128)S(1)} %get-tuple-element.5, f32[7168]{0:T(1024)S(1)} %copy-done.3, bf16[128,7168]{1,0:T(8,128)(2,1)S(1)} %copy-done, f32[128,7168]{1,0:T(8,128)S(1)} %get-tuple-element.10, f32[128]{0:T(128)S(1)} %get-tuple-element.6, ...), kind=kLoop, calls=%fused_computation.61 | loop fusion | flops 9167872 | bytes 9233920 | tf_op jit(solution)/shard_map/reduce_sum | solution.py:134
  145.8 41.3 %psum.7 = f32[7168]{0:T(1024)} all-reduce(f32[7168]{0:T(1024)S(1)} %get-tuple-element.3), channel_id=1, replica_groups=mesh['dp'=4,'expert'=8] {'dp','expert'}, use_global_device_ids=true, to_apply=%region_10.11 | all-reduce | flops 7168 | bytes 57344 | tf_op jit(solution)/shard_map/psum | solution.py:134
  187.2 0.0 all-to-all-done.1
  187.2 0.1 convert_reduce_fusion.1
  187.3 4.4 %fusion.2 = bf16[128,7168]{1,0:T(8,128)(2,1)} fusion(f32[4,8,7168]{2,1,0:T(8,128)S(1)} %convert_reduce_fusion.1, bf16[128,7168]{1,0:T(8,128)(2,1)S(1)} %copy-done, f32[7168]{0:T(1024)S(1)} %copy-done.3, f32[128,4]{0,1:T(4,128)S(1)} %select_reduce_fusion.1, s32[128,4]{0,1:T(4,128)S(1)} %add_select_fusion), kind=kOutput, calls=%fused_computation.6 | convolution fusion | flops 355999744 | bytes 4620288 | tf_op jit(solution)/shard_map/dot_general | solution.py:75
  (8 shorter events, 0.1 us)
Async XLA Ops:
  106.3 27.2 %all-to-all-start.2 = ((bf16[8,8,7168]{2,1,0:T(8,128)(2,1)}), bf16[8,8,7168]{2,1,0:T(8,128)(2,1)S(1)}, u32[]{:S(2)}, u32[]{:S(2)}) async-start(bf16[8,8,7168]{2,1,0:T(8,128)(2,1)} %fusion.5), calls=%async_computation.2 | async-start | bytes 1835008 | tf_op jit(solution)/shard_map/all_to_all | solution.py:113
  109.8 28.2 %copy-start.6 = (s32[128,8]{0,1:T(8,128)S(1)}, s32[128,8]{0,1:T(8,128)}, u32[]{:S(2)}) copy-start(s32[128,8]{0,1:T(8,128)} %param.13) | copy-start | bytes 12292
  109.8 28.2 %copy-start.5 = (s32[128,8]{0,1:T(8,128)S(1)}, s32[128,8]{0,1:T(8,128)}, u32[]{:S(2)}) copy-start(s32[128,8]{0,1:T(8,128)} %param.12) | copy-start | bytes 12292
  118.6 20.9 %copy-start = (bf16[128,7168]{1,0:T(8,128)(2,1)S(1)}, bf16[128,7168]{1,0:T(8,128)(2,1)}, u32[]{:S(2)}) copy-start(bf16[128,7168]{1,0:T(8,128)(2,1)} %param.9) | copy-start | bytes 5505028
  118.6 20.9 %copy-start.3 = (f32[7168]{0:T(1024)S(1)}, f32[7168]{0:T(1024)}, u32[]{:S(2)}) copy-start(f32[7168]{0:T(1024)} %param.10) | copy-start | bytes 86020
  118.6 20.9 %copy-start.4 = (f32[7168]{0:T(1024)S(1)}, f32[7168]{0:T(1024)}, u32[]{:S(2)}) copy-start(f32[7168]{0:T(1024)} %param.11) | copy-start | bytes 86020
  133.5 0.9 copy-start.2
  134.4 52.7 %all-to-all-start.1 = ((bf16[8,8,7168]{2,1,0:T(8,128)(2,1)}), bf16[8,8,7168]{2,1,0:T(8,128)(2,1)S(1)}, u32[]{:S(2)}, u32[]{:S(2)}) async-start(bf16[8,8,7168]{2,1,0:T(8,128)(2,1)} %fusion.4), calls=%async_computation.1 | async-start | bytes 1835008 | tf_op jit(solution)/shard_map/all_to_all | solution.py:105
  139.5 3.7 %copy-start.1 = (bf16[128,7168]{1,0:T(8,128)(2,1)S(1)}, bf16[128,7168]{1,0:T(8,128)(2,1)}, u32[]{:S(2)}) copy-start(bf16[128,7168]{1,0:T(8,128)(2,1)} %param.17) | copy-start | bytes 5505028
where the time goes:
time: 192 us
  blocking collectives  90.9 us (47%)
  matrix products  62.8 us (33%)
  waiting for transfers between devices  14.9 us (8%)
  other arithmetic  9.82 us (5%)
  starting transfers between devices  7.11 us (4%)
  local copies, waits for them, and re-layouts  5.27 us (3%)
    all_to_all x1, blocking collectives, shards(): lax.all_to_all(sending, 'expert', split_axis=0, concat_axis=0, tiled=True)  49.6 us
    psum x1, blocking collectives, shards(): steer_grad = lax.psum(jnp.sum(total_grad, axis=0), ('dp', 'expert'))  41.3 us
    all_to_all x1, waiting for transfers between devices, shards(): lax.all_to_all(backward.reshape(expert_count, capacity, feature_count), '...  14.9 us
    dot_general x1, matrix products, share_backward(): lax.dot_general(back_up, up_cols, contract, preferred_element_type=jnp.fl...  10.9 us
    dot_general x1, matrix products, share_backward(): lax.dot_general(back_gate, gate_cols, contract, preferred_element_type=jn...  9.73 us
    dot_general x1, matrix products, share_backward(): lax.dot_general(grad_rows, down_rows, contract, preferred_element_type=jn...  9.72 us
    dot_general x1, matrix products, share_forward(): jnp.dot(hidden, down_rows, preferred_element_type=jnp.float32)  8.77 us
    dot_general x2, matrix products, apply_combine(): return jnp.dot(combine, partial_sums, precision=lax.Precision.HIGHEST)  8 us
  transfers between devices with their start and end apart: 2, of which 1 were waited for; matrix products, arithmetic and copies ran while one was open for 9% of the time, Pallas kernels for 0%

commit v1 on v0

--- a/solution.py
+++ b/solution.py
@@ -7,6 +7,24 @@
 CAP = 8
 EPSILON = 1e-06
 GATE_UNIT = 1.0 / 65536.0
+
+
+def play_waves_on_mesh(unit):
+    mat_out, value_now = (jax.lax.axis_size("expert"), jax.lax.axis_index("expert"))
+    after = unit.shape[0] // mat_out
+    piece_now = list(unit.shape)
+    piece_now[0] = after
+    v_next = piece_now[0]
+    piece_now[0] = v_next * mat_out
+    everything = jnp.zeros(piece_now, unit.dtype)
+    for tick in range(mat_out):
+        z2 = lax.dynamic_slice_in_dim(unit, (value_now ^ tick) * after, after, axis=0)
+        if tick:
+            z2 = jax.lax.ppermute(z2, "expert", list(map(lambda h: (h, h ^ tick), range(mat_out))))
+        everything = lax.dynamic_update_slice_in_dim(
+            everything, z2, (value_now ^ tick) * v_next, axis=0
+        )
+    return everything
 
 
 def slot_tables(route_ids, route_gates, flight, capacity):
@@ -98,7 +116,7 @@
         axis=1,
     )
     sending = jnp.repeat(packed, group_size, axis=0)
-    arrived = lax.all_to_all(sending, "expert", split_axis=0, concat_axis=0, tiled=True)
+    arrived = play_waves_on_mesh(sending)
     local_rows = arrived[:, 0].reshape(expert_count * capacity, feature_count)
     local_grads = arrived[:, 1].reshape(expert_count * capacity, feature_count)
     forward, gate_pre, up_pre = share_forward(local_rows, gate_weight, up_weight, down_weight)

time: 192 us -> 185 us (0.964)
  blocking collectives: 90.9 us -> 41.1 us
  waiting for transfers between devices: 14.9 us -> 40.5 us
  starting transfers between devices: 7.11 us -> 28.1 us
  matrix products: 62.8 us -> 58 us
    all_to_all x1 -> x0, blocking collectives: 49.6 us -> none  [shards(): lax.all_to_all(sending, 'expert', split_axis=0, concat_axis=0, tiled=True)]
    ppermute x0 -> x7, waiting for transfers between devices: none -> 25.6 us  [play_waves_on_mesh(): jax.lax.ppermute(z2, 'expert', list(map(lambda h: (h, h ^ tick), range(ma...]
    all_to_all x1, starting transfers between devices: 3.55 us -> 14.3 us  [shards(): lax.all_to_all(backward.reshape(expert_count, capacity, feature_count), '...]
    ppermute x0 -> x7, starting transfers between devices: none -> 10 us  [play_waves_on_mesh(): jax.lax.ppermute(z2, 'expert', list(map(lambda h: (h, h ^ tick), range(ma...]
    dot_general x1, matrix products: 7.85 us -> 2.68 us  [share_forward(): jnp.dot(token_rows, gate_cols, preferred_element_type=jnp.float32)]
  transfers between devices with their start and end apart: 2 -> 9, of which waited for: 1 -> 6; matrix products, arithmetic and copies ran while one was open for 9% -> 9% of each run, Pallas kernels for 0% -> 0%
where the time goes in v1:
time: 185 us; the launch traced here: 184 us
  matrix products  58 us (31%)
  blocking collectives  41.1 us (22%)
  waiting for transfers between devices  40.5 us (22%)
  starting transfers between devices  28.1 us (15%)
  other arithmetic  9.82 us (5%)
  local copies, waits for them, and re-layouts  5.77 us (3%)
    psum x1, blocking collectives, shards(): steer_grad = lax.psum(jnp.sum(total_grad, axis=0), ('dp', 'expert'))  41.1 us
    ppermute x7, waiting for transfers between devices, play_waves_on_mesh(): jax.lax.ppermute(z2, 'expert', list(map(lambda h: (h, h ^ tick), range(ma...  25.6 us
    all_to_all x1, waiting for transfers between devices, shards(): lax.all_to_all(backward.reshape(expert_count, capacity, feature_count), '...  14.9 us
    all_to_all x1, starting transfers between devices, shards(): lax.all_to_all(backward.reshape(expert_count, capacity, feature_count), '...  14.3 us
    dot_general x1, matrix products, share_backward(): lax.dot_general(back_up, up_cols, contract, preferred_element_type=jnp.fl...  10.7 us
    ppermute x7, starting transfers between devices, play_waves_on_mesh(): jax.lax.ppermute(z2, 'expert', list(map(lambda h: (h, h ^ tick), range(ma...  10 us
    dot_general x1, matrix products, share_backward(): lax.dot_general(back_gate, gate_cols, contract, preferred_element_type=jn...  9.93 us
    dot_general x1, matrix products, share_backward(): lax.dot_general(grad_rows, down_rows, contract, preferred_element_type=jn...  9.88 us
  transfers between devices with their start and end apart: 9, of which 6 were waited for; matrix products, arithmetic and copies ran while one was open for 9% of the time, Pallas kernels for 0%

profile of v1, /device:TPU:0, one launch (start us, length us, event | category | flops | bytes accessed | tf_op | source)
XLA Modules:
  0.0 184.3 jit_solution(13174777172779912769)
XLA Ops:
  0.6 0.7 fusion.16
  1.3 0.1 copy.20
  1.5 0.2 reduce_window_sum.11
  1.6 0.1 copy.21
  1.7 0.2 select_reduce_fusion
  1.9 0.2 fusion.15
  2.1 0.1 reshape.94
  2.2 2.1 %multiply_reduce_fusion.1 = f32[128]{0:T(128)S(1)} fusion(bf16[128,7168]{1,0:T(8,128)(2,1)} %param.9, f32[7168]{0:T(1024)} %param.10), kind=kLoop, calls=%fused_computation.15 | loop fusion | flops 3669888 | bytes 1864192 | tf_op jit(solution)/shard_map/reduce_sum | solution.py:55
  4.2 2.1 %multiply_convert_fusion = bf16[128,7168]{1,0:T(8,128)(2,1)S(1)} fusion(bf16[128,7168]{1,0:T(8,128)(2,1)} %param.9, f32[7168]{0:T(1024)} %param.11, f32[128]{0:T(128)S(1)} %get-tuple-element.14, f32[7168]{0:T(1024)} %param.10), kind=kLoop, calls=%fused_computation.14 | loop fusion | flops 4587520 | bytes 3727872 | tf_op jit(solution)/shard_map/convert_element_type | solution.py:56
  6.3 0.8 gather_fusion
  7.2 3.0 %gather_fusion.1 = bf16[32,7168]{1,0:T(8,128)(2,1)S(1)} fusion(bf16[128,7168]{1,0:T(8,128)(2,1)} %param.17, s32[1024]{0:T(1024)S(1)} %pad_clamp_fusion), kind=kCustom, calls=%fused_computation.1 | custom fusion | bytes 917632 | tf_op jit(solution)/shard_map/gather | solution.py:49
  10.2 0.1 bitcast_select_fusion.1
  10.3 0.1 pad_maximum_fusion
  10.4 0.1 copy.22
  10.5 0.2 broadcast_in_dim.88
  10.7 0.2 broadcast_in_dim.83
  10.9 0.2 constant_dynamic-slice_fusion.6
  11.0 0.6 collective-permute-start
  11.6 2.6 %collective-permute-start.1 = (bf16[1,2,8,7168]{3,2,1,0:T(8,128)(2,1)S(1)}, bf16[1,2,8,7168]{3,2,1,0:T(8,128)(2,1)S(1)}, u32[]{:S(2)}, u32[]{:S(2)}) collective-permute-start(bf16[1,2,8,7168]{3,2,1,0:T(8,128)(2,1)S(1)} %get-tuple-element.10), channel_id=1, source_target_pairs={{0,2},{1,3},{2,0},{3,1},{4,6},{5,7},{6,4},{7,5},{8,10},{9,11},{10,... | collective-permute-start | bytes 688136 | tf_op jit(solution)/shard_map/ppermute | solution.py:23
  14.2 0.0 collective-permute-start.2
  14.3 2.8 %collective-permute-start.3 = (bf16[1,2,8,7168]{3,2,1,0:T(8,128)(2,1)S(1)}, bf16[1,2,8,7168]{3,2,1,0:T(8,128)(2,1)S(1)}, u32[]{:S(2)}, u32[]{:S(2)}) collective-permute-start(bf16[1,2,8,7168]{3,2,1,0:T(8,128)(2,1)S(1)} %get-tuple-element.8), channel_id=1, source_target_pairs={{0,4},{1,5},{2,6},{3,7},{4,0},{5,1},{6,2},{7,3},{8,12},{9,13},{10,... | collective-permute-start | bytes 688136 | tf_op jit(solution)/shard_map/ppermute | solution.py:23
  17.0 3.6 %collective-permute-start.5 = (bf16[1,2,8,7168]{3,2,1,0:T(8,128)(2,1)S(1)}, bf16[1,2,8,7168]{3,2,1,0:T(8,128)(2,1)S(1)}, u32[]{:S(2)}, u32[]{:S(2)}) collective-permute-start(bf16[1,2,8,7168]{3,2,1,0:T(8,128)(2,1)S(1)} %get-tuple-element.6), channel_id=1, source_target_pairs={{0,6},{1,7},{2,4},{3,5},{4,2},{5,3},{6,0},{7,1},{8,14},{9,15},{10,... | collective-permute-start | bytes 688136 | tf_op jit(solution)/shard_map/ppermute | solution.py:23
  20.7 9.4 %collective-permute-done.1 = bf16[1,2,8,7168]{3,2,1,0:T(8,128)(2,1)S(1)} collective-permute-done((bf16[1,2,8,7168]{3,2,1,0:T(8,128)(2,1)S(1)}, bf16[1,2,8,7168]{3,2,1,0:T(8,128)(2,1)S(1)}, u32[]{:S(2)}, u32[]{:S(2)}) %collective-permute-start.1) | collective-permute-done | bytes 229408 | tf_op jit(solution)/shard_map/ppermute | solution.py:23
  30.0 0.4 collective-permute-start.6
  30.5 4.0 %collective-permute-done.2 = bf16[1,2,8,7168]{3,2,1,0:T(8,128)(2,1)S(1)} collective-permute-done((bf16[1,2,8,7168]{3,2,1,0:T(8,128)(2,1)S(1)}, bf16[1,2,8,7168]{3,2,1,0:T(8,128)(2,1)S(1)}, u32[]{:S(2)}, u32[]{:S(2)}) %collective-permute-start.2) | collective-permute-done | bytes 229408 | tf_op jit(solution)/shard_map/ppermute | solution.py:23
  34.5 0.5 collective-permute-done.4
  35.1 7.9 %collective-permute-done.5 = bf16[1,2,8,7168]{3,2,1,0:T(8,128)(2,1)S(1)} collective-permute-done((bf16[1,2,8,7168]{3,2,1,0:T(8,128)(2,1)S(1)}, bf16[1,2,8,7168]{3,2,1,0:T(8,128)(2,1)S(1)}, u32[]{:S(2)}, u32[]{:S(2)}) %collective-permute-start.5) | collective-permute-done | bytes 229408 | tf_op jit(solution)/shard_map/ppermute | solution.py:23
  43.0 3.8 %collective-permute-done.6 = bf16[1,2,8,7168]{3,2,1,0:T(8,128)(2,1)S(1)} collective-permute-done((bf16[1,2,8,7168]{3,2,1,0:T(8,128)(2,1)S(1)}, bf16[1,2,8,7168]{3,2,1,0:T(8,128)(2,1)S(1)}, u32[]{:S(2)}, u32[]{:S(2)}) %collective-permute-start.6) | collective-permute-done | bytes 229408 | tf_op jit(solution)/shard_map/ppermute | solution.py:23
  46.8 0.0 slice-start
  46.8 9.9 %fusion.6 = f32[64,1024]{1,0:T(8,128)S(1)} fusion(bf16[1024,7168]{1,0:T(8,128)(2,1)} %param.16, bf16[8,2,8,7168]{3,2,1,0:T(8,128)(2,1)S(1)} %constant_dynamic-update-slice_fusion.6), kind=kOutput, calls=%fused_computation.20 | convolution fusion | flops 939524096 | bytes 15859712 | tf_op jit(solution)/shard_map/dot_general | solution.py:77
  56.7 0.0 slice-start.3
  56.7 8.0 %fusion.7 = f32[64,1024]{1,0:T(8,128)S(1)} fusion(bf16[7168,1024]{1,0:T(8,128)(2,1)} %param.15, bf16[8,2,8,7168]{3,2,1,0:T(8,128)(2,1)S(1)} %constant_dynamic-update-slice_fusion.6), kind=kOutput, calls=%fused_computation.23 | convolution fusion | flops 939524096 | bytes 15859712 | tf_op jit(solution)/shard_map/dot_general | solution.py:69
  64.8 2.7 %fusion.8 = f32[64,1024]{1,0:T(8,128)S(1)} fusion(bf16[7168,1024]{1,0:T(8,128)(2,1)S(1)} %bitcast.45, bf16[8,2,8,7168]{3,2,1,0:T(8,128)(2,1)S(1)} %constant_dynamic-update-slice_fusion.6), kind=kOutput, calls=%fused_computation.24 | convolution fusion | flops 939524096 | bytes 15859712 | tf_op jit(solution)/shard_map/dot_general | solution.py:68
  67.5 9.9 %fusion.9 = f32[64,7168]{1,0:T(8,128)S(1)} fusion(bf16[7168,1024]{1,0:T(8,128)(2,1)} %param.14, f32[64,1024]{1,0:T(8,128)S(1)} %fusion.8, f32[64,1024]{1,0:T(8,128)S(1)} %fusion.6, f32[64,1024]{1,0:T(8,128)S(1)} %fusion.7), kind=kOutput, calls=%fused_computation.32 | convolution fusion | flops 940179456 | bytes 17301504 | tf_op jit(solution)/shard_map/dot_general | solution.py:85
  77.4 10.7 %fusion.5 = bf16[8,8,7168]{2,1,0:T(8,128)(2,1)} fusion(f32[64,7168]{1,0:T(8,128)S(1)} %fusion.9, bf16[7168,1024]{1,0:T(8,128)(2,1)} %param.15, f32[64,1024]{1,0:T(8,128)S(1)} %fusion.6, f32[64,1024]{1,0:T(8,128)S(1)} %fusion.8), kind=kOutput, calls=%fused_computation.11 | convolution fusion | flops 940834816 | bytes 17956864 | tf_op jit(solution)/shard_map/dot_general | solution.py:86
  88.1 14.3 %all-to-all-start.1 = ((bf16[8,8,7168]{2,1,0:T(8,128)(2,1)}), bf16[8,8,7168]{2,1,0:T(8,128)(2,1)S(1)}, u32[]{:S(2)}, u32[]{:S(2)}) async-start(bf16[8,8,7168]{2,1,0:T(8,128)(2,1)} %fusion.5), calls=%async_computation.1 | async-start | bytes 1835008 | tf_op jit(solution)/shard_map/all_to_all | solution.py:131
  102.4 0.0 copy-start.5
  102.4 8.8 %fusion.4 = bf16[8,8,7168]{2,1,0:T(8,128)(2,1)} fusion(bf16[1024,7168]{1,0:T(8,128)(2,1)} %param.16, f32[64,1024]{1,0:T(8,128)S(1)} %fusion.7, f32[64,1024]{1,0:T(8,128)S(1)} %fusion.8), kind=kOutput, calls=%fused_computation.10 | convolution fusion | flops 940376064 | bytes 16121856 | tf_op jit(solution)/shard_map/dot_general | solution.py:71
  111.2 14.9 %all-to-all-done.1 = bf16[8,8,7168]{2,1,0:T(8,128)(2,1)S(1)} async-done(((bf16[8,8,7168]{2,1,0:T(8,128)(2,1)}), bf16[8,8,7168]{2,1,0:T(8,128)(2,1)S(1)}, u32[]{:S(2)}, u32[]{:S(2)}) %all-to-all-start.1) | async-done | bytes 917536 | tf_op jit(solution)/shard_map/all_to_all | solution.py:131
  126.2 0.9 copy-done.2
  127.1 3.8 %all-to-all-start = ((bf16[8,8,7168]{2,1,0:T(8,128)(2,1)}), bf16[8,8,7168]{2,1,0:T(8,128)(2,1)S(1)}, u32[]{:S(2)}, u32[]{:S(2)}) async-start(bf16[8,8,7168]{2,1,0:T(8,128)(2,1)} %fusion.4), calls=%async_computation | async-start | bytes 1835008 | tf_op jit(solution)/shard_map/all_to_all | solution.py:123
  130.9 1.4 convert_reduce_fusion
  132.4 0.0 copy-start.1
  132.4 3.7 %multiply_reduce_fusion = (f32[128]{0:T(128)S(1)}, f32[128,7168]{1,0:T(8,128)S(1)}) fusion(bf16[128,7168]{1,0:T(8,128)(2,1)S(1)} %copy-done, f32[7168]{0:T(1024)S(1)} %copy-done.3, f32[7168]{0:T(1024)S(1)} %copy-done.4, f32[4,8,7168]{2,1,0:T(8,128)S(1)} %convert_reduce_fusion, f32[128,4]{0,1:T(4,128)S(1)} %select_reduce_fusion.1, ...), kind=kOutput, calls=%fused_computation.13 | convolution fusion | flops 356917120 | bytes 6484480 | tf_op jit(solution)/shard_map/dot_general | solution.py:93
  136.1 2.6 %fusion.28 = (f32[7168]{0:T(1024)S(1)}, bf16[128,7168]{1,0:T(8,128)(2,1)}) fusion(f32[128]{0:T(128)S(1)} %broadcast_multiply_fusion, f32[128]{0:T(128)S(1)} %get-tuple-element.13, f32[7168]{0:T(1024)S(1)} %copy-done.3, bf16[128,7168]{1,0:T(8,128)(2,1)S(1)} %copy-done, f32[128,7168]{1,0:T(8,128)S(1)} %get-tuple-element.18, f32[128]{0:T(128)S(1)} %get-tuple-element.14, ...), kind=kLoop, calls=%fused_computation.76 | loop fusion | flops 9167872 | bytes 9233920 | tf_op jit(solution)/shard_map/reduce_sum | solution.py:152
  138.7 41.1 %psum.7 = f32[7168]{0:T(1024)} all-reduce(f32[7168]{0:T(1024)S(1)} %get-tuple-element.3), channel_id=1, replica_groups=mesh['dp'=4,'expert'=8] {'dp','expert'}, use_global_device_ids=true, to_apply=%region_10.11 | all-reduce | flops 7168 | bytes 57344 | tf_op jit(solution)/shard_map/psum | solution.py:152
  179.8 0.1 convert_reduce_fusion.1
  179.9 4.3 %fusion.2 = bf16[128,7168]{1,0:T(8,128)(2,1)} fusion(f32[4,8,7168]{2,1,0:T(8,128)S(1)} %convert_reduce_fusion.1, bf16[128,7168]{1,0:T(8,128)(2,1)S(1)} %copy-done, f32[7168]{0:T(1024)S(1)} %copy-done.3, f32[128,4]{0,1:T(4,128)S(1)} %select_reduce_fusion.1, s32[128,4]{0,1:T(4,128)S(1)} %add_select_fusion), kind=kOutput, calls=%fused_computation.6 | convolution fusion | flops 355999744 | bytes 4620288 | tf_op jit(solution)/shard_map/dot_general | solution.py:93
  (37 shorter events, 0.2 us)
Async XLA Ops:
  11.0 6.0 %collective-permute-start = (bf16[1,2,8,7168]{3,2,1,0:T(8,128)(2,1)S(1)}, bf16[1,2,8,7168]{3,2,1,0:T(8,128)(2,1)S(1)}, u32[]{:S(2)}, u32[]{:S(2)}) collective-permute-start(bf16[1,2,8,7168]{3,2,1,0:T(8,128)(2,1)S(1)} %get-tuple-element.11), channel_id=1, source_target_pairs={{0,1},{1,0},{2,3},{3,2},{4,5},{5,4},{6,7},{7,6},{8,9},{9,8},{10,11... | collective-permute-start | bytes 688136 | tf_op jit(solution)/shard_map/ppermute | solution.py:23
  11.6 18.4 %collective-permute-start.1 = (bf16[1,2,8,7168]{3,2,1,0:T(8,128)(2,1)S(1)}, bf16[1,2,8,7168]{3,2,1,0:T(8,128)(2,1)S(1)}, u32[]{:S(2)}, u32[]{:S(2)}) collective-permute-start(bf16[1,2,8,7168]{3,2,1,0:T(8,128)(2,1)S(1)} %get-tuple-element.10), channel_id=1, source_target_pairs={{0,2},{1,3},{2,0},{3,1},{4,6},{5,7},{6,4},{7,5},{8,10},{9,11},{10,... | collective-permute-start | bytes 688136 | tf_op jit(solution)/shard_map/ppermute | solution.py:23
  14.2 20.2 %collective-permute-start.2 = (bf16[1,2,8,7168]{3,2,1,0:T(8,128)(2,1)S(1)}, bf16[1,2,8,7168]{3,2,1,0:T(8,128)(2,1)S(1)}, u32[]{:S(2)}, u32[]{:S(2)}) collective-permute-start(bf16[1,2,8,7168]{3,2,1,0:T(8,128)(2,1)S(1)} %get-tuple-element.9), channel_id=1, source_target_pairs={{0,3},{1,2},{2,1},{3,0},{4,7},{5,6},{6,5},{7,4},{8,11},{9,10},{10,... | collective-permute-start | bytes 688136 | tf_op jit(solution)/shard_map/ppermute | solution.py:23
  14.3 20.2 %collective-permute-start.3 = (bf16[1,2,8,7168]{3,2,1,0:T(8,128)(2,1)S(1)}, bf16[1,2,8,7168]{3,2,1,0:T(8,128)(2,1)S(1)}, u32[]{:S(2)}, u32[]{:S(2)}) collective-permute-start(bf16[1,2,8,7168]{3,2,1,0:T(8,128)(2,1)S(1)} %get-tuple-element.8), channel_id=1, source_target_pairs={{0,4},{1,5},{2,6},{3,7},{4,0},{5,1},{6,2},{7,3},{8,12},{9,13},{10,... | collective-permute-start | bytes 688136 | tf_op jit(solution)/shard_map/ppermute | solution.py:23
  17.0 18.0 %collective-permute-start.4 = (bf16[1,2,8,7168]{3,2,1,0:T(8,128)(2,1)S(1)}, bf16[1,2,8,7168]{3,2,1,0:T(8,128)(2,1)S(1)}, u32[]{:S(2)}, u32[]{:S(2)}) collective-permute-start(bf16[1,2,8,7168]{3,2,1,0:T(8,128)(2,1)S(1)} %get-tuple-element.7), channel_id=1, source_target_pairs={{0,5},{1,4},{2,7},{3,6},{4,1},{5,0},{6,3},{7,2},{8,13},{9,12},{10,... | collective-permute-start | bytes 688136 | tf_op jit(solution)/shard_map/ppermute | solution.py:23
  17.0 25.9 %collective-permute-start.5 = (bf16[1,2,8,7168]{3,2,1,0:T(8,128)(2,1)S(1)}, bf16[1,2,8,7168]{3,2,1,0:T(8,128)(2,1)S(1)}, u32[]{:S(2)}, u32[]{:S(2)}) collective-permute-start(bf16[1,2,8,7168]{3,2,1,0:T(8,128)(2,1)S(1)} %get-tuple-element.6), channel_id=1, source_target_pairs={{0,6},{1,7},{2,4},{3,5},{4,2},{5,3},{6,0},{7,1},{8,14},{9,15},{10,... | collective-permute-start | bytes 688136 | tf_op jit(solution)/shard_map/ppermute | solution.py:23
  30.0 16.7 %collective-permute-start.6 = (bf16[1,2,8,7168]{3,2,1,0:T(8,128)(2,1)S(1)}, bf16[1,2,8,7168]{3,2,1,0:T(8,128)(2,1)S(1)}, u32[]{:S(2)}, u32[]{:S(2)}) collective-permute-start(bf16[1,2,8,7168]{3,2,1,0:T(8,128)(2,1)S(1)} %get-tuple-element.5), channel_id=1, source_target_pairs={{0,7},{1,6},{2,5},{3,4},{4,3},{5,2},{6,1},{7,0},{8,15},{9,14},{10,... | collective-permute-start | bytes 688136 | tf_op jit(solution)/shard_map/ppermute | solution.py:23
  46.8 17.9 %slice-start = ((s8[14680064]{0:T(1024)(128)(4,1)}), s8[4194304]{0:T(1024)(128)(4,1)S(1)}, s32[]{:S(2)}) async-start(s8[14680064]{0:T(1024)(128)(4,1)} %bitcast.44), calls=%async_computation.2 | async-start | bytes 8388608
  46.8 17.9 %slice-start.1 = ((s8[14680064]{0:T(1024)(128)(4,1)}), s8[2097152]{0:T(1024)(128)(4,1)S(1)}, s32[]{:S(2)}) async-start(s8[14680064]{0:T(1024)(128)(4,1)} %bitcast.44), calls=%async_computation.3 | async-start | bytes 4194304
  56.7 8.1 %slice-start.2 = ((s8[14680064]{0:T(1024)(128)(4,1)}), s8[4194304]{0:T(1024)(128)(4,1)S(1)}, s32[]{:S(2)}) async-start(s8[14680064]{0:T(1024)(128)(4,1)} %bitcast.44), calls=%async_computation.4 | async-start | bytes 8388608
  56.7 8.1 %slice-start.3 = ((s8[14680064]{0:T(1024)(128)(4,1)}), s8[4194304]{0:T(1024)(128)(4,1)S(1)}, s32[]{:S(2)}) async-start(s8[14680064]{0:T(1024)(128)(4,1)} %bitcast.44), calls=%async_computation.5 | async-start | bytes 8388608
  88.1 38.1 %all-to-all-start.1 = ((bf16[8,8,7168]{2,1,0:T(8,128)(2,1)}), bf16[8,8,7168]{2,1,0:T(8,128)(2,1)S(1)}, u32[]{:S(2)}, u32[]{:S(2)}) async-start(bf16[8,8,7168]{2,1,0:T(8,128)(2,1)} %fusion.5), calls=%async_computation.1 | async-start | bytes 1835008 | tf_op jit(solution)/shard_map/all_to_all | solution.py:131
  102.4 28.5 %copy-start.6 = (s32[128,8]{0,1:T(8,128)S(1)}, s32[128,8]{0,1:T(8,128)}, u32[]{:S(2)}) copy-start(s32[128,8]{0,1:T(8,128)} %param.13) | copy-start | bytes 12292
  102.4 28.5 %copy-start.5 = (s32[128,8]{0,1:T(8,128)S(1)}, s32[128,8]{0,1:T(8,128)}, u32[]{:S(2)}) copy-start(s32[128,8]{0,1:T(8,128)} %param.12) | copy-start | bytes 12292
  111.2 21.2 %copy-start = (bf16[128,7168]{1,0:T(8,128)(2,1)S(1)}, bf16[128,7168]{1,0:T(8,128)(2,1)}, u32[]{:S(2)}) copy-start(bf16[128,7168]{1,0:T(8,128)(2,1)} %param.9) | copy-start | bytes 5505028
  111.2 21.2 %copy-start.3 = (f32[7168]{0:T(1024)S(1)}, f32[7168]{0:T(1024)}, u32[]{:S(2)}) copy-start(f32[7168]{0:T(1024)} %param.10) | copy-start | bytes 86020
  111.2 21.2 %copy-start.4 = (f32[7168]{0:T(1024)S(1)}, f32[7168]{0:T(1024)}, u32[]{:S(2)}) copy-start(f32[7168]{0:T(1024)} %param.11) | copy-start | bytes 86020
  126.2 0.9 copy-start.2
  127.1 52.7 %all-to-all-start = ((bf16[8,8,7168]{2,1,0:T(8,128)(2,1)}), bf16[8,8,7168]{2,1,0:T(8,128)(2,1)S(1)}, u32[]{:S(2)}, u32[]{:S(2)}) async-start(bf16[8,8,7168]{2,1,0:T(8,128)(2,1)} %fusion.4), calls=%async_computation | async-start | bytes 1835008 | tf_op jit(solution)/shard_map/all_to_all | solution.py:123
  132.4 3.7 %copy-start.1 = (bf16[128,7168]{1,0:T(8,128)(2,1)S(1)}, bf16[128,7168]{1,0:T(8,128)(2,1)}, u32[]{:S(2)}) copy-start(bf16[128,7168]{1,0:T(8,128)(2,1)} %param.17) | copy-start | bytes 5505028
